TPU v7x, 256 devices: a whole 4x4x8 slice. The times are simulated.
256 devices in a mesh: row: 16 (over x_lo, z), col: 16 (over x_hi, y, core).
Axes of the slice: x: 4 (x_hi: 2, x_lo: 2; x = x_hi * 2 + x_lo), y: 4, z: 8, core: 2. Of those that a mesh axis runs over, the one named last changes fastest.
Arguments:
- sp2_branch: int32 [3], replicated, may hold values from 0 to 1, as said below
- p0_occupancy: int32 [32, 32], replicated, may hold values from 0 to 1, as said below
- p1_occupancy: int32 [32, 32], replicated, may hold values from 0 to 1, as said below
- p0_columns: bfloat16 [73728, 512], P('col'), as said below
- p1_tiles: bfloat16 [3, 8192, 8192], P(None, 'row', 'col'), may hold values from -6 to 6, as said below
Outputs:
- p1_next: bfloat16 [3, 8192, 8192], P(None, 'row', 'col')
Inputs may be any that keep to these rules, and one draw needn't show every extreme that they name: `sp2_branch`: both values occur among the displacements. `p0_occupancy`: symmetric; every diagonal block is 1; blocks more than 8 apart around the circle of 32 blocks are 0. `p1_occupancy`: symmetric. `p0_columns`: the strips describe one symmetric matrix: a stored entry at row u and column v equals the stored entry at row v and column u; blocks more than 8 apart around the circle are zero. `p1_tiles`: each displacement's matrix is symmetric.
All inputs are finite; a program needn't handle non-finite values.
Results may differ from a plain program's by a relative error of at most 0.001.
Values may be sent and summed in bfloat16 or wider, within the bound.
No kernel may reach another device: no remote copies, remote signals or barrier semaphores. Data moves between devices by JAX's collectives and lax.ppermute only.
A program may use at most 192 MiB of HBM per device.

v0:
```python
import jax
import jax.numpy as jnp
from jax import lax
from jax.sharding import PartitionSpec as P

BLK = 256


def from_behind(array, axis, by):
    length = lax.axis_size(axis)
    return lax.ppermute(array, axis, [(i, (i + by) % length) for i in range(length)])


def broadcast(array, axis, root):
    mine = lax.axis_index(axis) == root
    return lax.psum(jnp.where(mine, array, jnp.zeros_like(array)), axis)


def mask_blocks(values, occupancy):
    leading = values.shape[:-2]
    row_blocks = values.shape[-2] // BLK
    col_blocks = values.shape[-1] // BLK
    shaped = values.reshape(leading + (row_blocks, BLK, col_blocks, BLK))
    weight = occupancy.astype(values.dtype)[:, None, :, None]
    return (shaped * weight).reshape(values.shape)


def right_product(left_op, right_op):
    return jnp.einsum("drc,ck->drk", left_op, right_op, preferred_element_type=jnp.float32)


def left_product(left_op, right_op):
    return jnp.einsum("kr,dkc->drc", left_op, right_op, preferred_element_type=jnp.float32)


def column_term(summed, incoming, factor):
    return summed + right_product(incoming, factor)


def row_term(summed, incoming, factor):
    return summed + left_product(factor, incoming)


def col_move(values, distance):
    return from_behind(values, "col", distance)


def row_move(values, distance):
    return from_behind(values, "row", distance)


def body(sp2_branch, p0_occupancy, p1_occupancy, p0_columns, p1_tiles):
    col_count = lax.axis_size("col")
    col_width = p0_columns.shape[1]
    row_height = p1_tiles.shape[1]
    col_blocks = col_width // BLK
    row_blocks = row_height // BLK
    strip_blocks = p0_columns.shape[0] // BLK
    band_half = (strip_blocks - col_blocks) // 2
    all_blocks = col_blocks * col_count
    col_span = band_half // col_blocks
    row_span = band_half // row_blocks
    row_at = lax.axis_index("row")
    col_at = lax.axis_index("col")
    own_occ = lax.dynamic_slice(
        p1_occupancy, (row_at * row_blocks, col_at * col_blocks), (row_blocks, col_blocks)
    )
    p1_local = mask_blocks(p1_tiles, own_occ)
    tripled = jnp.concatenate([p0_occupancy, p0_occupancy, p0_occupancy], axis=0)
    strip_occ = lax.dynamic_slice(
        tripled,
        (col_at * col_blocks - band_half + all_blocks, col_at * col_blocks),
        (strip_blocks, col_blocks),
    )
    strip_local = mask_blocks(p0_columns, strip_occ)

    def col_add(summed, incoming, distance):
        factor = strip_local[
            (distance + col_span) * col_width : (distance + col_span + 1) * col_width, :
        ]
        return column_term(summed, incoming, factor)

    summed_col = jnp.zeros(p1_local.shape, jnp.float32)
    summed_col = col_add(summed_col, p1_local, 0)
    moving = p1_local
    for distance in range(1, col_span + 1):
        moving = col_move(moving, 1)
        summed_col = col_add(summed_col, moving, -distance)
    moving = from_behind(moving, "col", -2 * col_span)
    summed_col = col_add(summed_col, moving, col_span)
    for distance in range(col_span - 1, 0, -1):
        moving = col_move(moving, 1)
        summed_col = col_add(summed_col, moving, distance)
    owner_col = row_at * row_blocks // col_blocks
    shared = broadcast(strip_local, "col", owner_col)

    def row_add(summed, incoming, distance):
        factor = shared[
            (distance + row_span) * row_height : (distance + row_span + 1) * row_height, :
        ]
        return row_term(summed, incoming, factor)

    summed_row = jnp.zeros(p1_local.shape, jnp.float32)
    summed_row = row_add(summed_row, p1_local, 0)
    moving = p1_local
    for distance in range(1, row_span + 1):
        moving = row_move(moving, 1)
        summed_row = row_add(summed_row, moving, -distance)
    moving = from_behind(moving, "row", -2 * row_span)
    summed_row = row_add(summed_row, moving, row_span)
    for distance in range(row_span - 1, 0, -1):
        moving = row_move(moving, 1)
        summed_row = row_add(summed_row, moving, distance)
    bracket = summed_col + summed_row
    squared = (sp2_branch == 1)[:, None, None]
    chosen = jnp.where(squared, bracket, 2.0 * p1_local.astype(jnp.float32) - bracket)
    return mask_blocks(chosen, own_occ).astype(jnp.bfloat16)


def solution(mesh):
    in_specs = (P(), P(), P(), P("col", None), P(None, "row", "col"))
    out_specs = P(None, "row", "col")
    return jax.shard_map(body, mesh=mesh, in_specs=in_specs, out_specs=out_specs, check_vma=False)
```

profile of v0, /device:TPU:2, one launch (start us, length us, event | category | flops | bytes accessed | tf_op | source)
XLA Modules:
  0.0 573.2 jit_solution(15829006812120409035)
XLA Ops:
  11.4 38.3 %collective-permute-done.8 = bf16[3,512,512]{2,1,0:T(8,128)(2,1)S(1)} collective-permute-done((bf16[3,512,512]{2,1,0:T(8,128)(2,1)S(1)}, bf16[3,512,512]{2,1,0:T(8,128)(2,1)S(1)}, u32[]{:S(2)}, u32[]{:S(2)}) %collective-permute-start.8) | collective-permute-done | bytes 1572896 | tf_op jit(solution)/shard_map/ppermute | solution.py:11
  49.7 52.7 %collective-permute-done = bf16[3,512,512]{2,1,0:T(8,128)(2,1)} collective-permute-done((bf16[3,512,512]{2,1,0:T(8,128)(2,1)S(1)}, bf16[3,512,512]{2,1,0:T(8,128)(2,1)}, u32[]{:S(2)}, u32[]{:S(2)}) %collective-permute-start) | collective-permute-done | bytes 1572896 | tf_op jit(solution)/shard_map/ppermute | solution.py:11
  106.2 53.6 %collective-permute-done.1 = bf16[3,512,512]{2,1,0:T(8,128)(2,1)} collective-permute-done((bf16[3,512,512]{2,1,0:T(8,128)(2,1)}, bf16[3,512,512]{2,1,0:T(8,128)(2,1)}, u32[]{:S(2)}, u32[]{:S(2)}) %collective-permute-start.1) | collective-permute-done | bytes 1572896 | tf_op jit(solution)/shard_map/ppermute | solution.py:11
  162.6 63.5 %collective-permute-done.2 = bf16[3,512,512]{2,1,0:T(8,128)(2,1)S(1)} collective-permute-done((bf16[3,512,512]{2,1,0:T(8,128)(2,1)}, bf16[3,512,512]{2,1,0:T(8,128)(2,1)S(1)}, u32[]{:S(2)}, u32[]{:S(2)}) %collective-permute-start.2) | collective-permute-done | bytes 1572896 | tf_op jit(solution)/shard_map/ppermute | solution.py:11
  226.1 8.0 %reshape.24 = bf16[18,256,2,256]{3,2,1,0:T(2,128)(2,1)} reshape(bf16[4608,512]{1,0:T(8,128)(2,1)} %param.8) | data formatting | bytes 9437184 | tf_op jit(solution)/shard_map/reshape | solution.py:23
  234.6 41.9 %collective-permute-done.3 = bf16[3,512,512]{2,1,0:T(8,128)(2,1)} collective-permute-done((bf16[3,512,512]{2,1,0:T(8,128)(2,1)S(1)}, bf16[3,512,512]{2,1,0:T(8,128)(2,1)}, u32[]{:S(2)}, u32[]{:S(2)}) %collective-permute-start.3) | collective-permute-done | bytes 1572896 | tf_op jit(solution)/shard_map/ppermute | solution.py:11
  279.1 8.6 %broadcast_multiply_fusion = bf16[18,256,2,256]{3,2,1,0:T(2,128)(2,1)} fusion(bf16[18,256,2,256]{3,2,1,0:T(2,128)(2,1)} %reshape.24, bf16[18,2]{1,0:T(8,128)(2,1)S(1)} %copy.27), kind=kLoop, calls=%fused_computation.5 | loop fusion | flops 2359296 | bytes 9437256 | tf_op jit(solution)/shard_map/mul | solution.py:25
  288.2 6.1 %fusion.13 = (bf16[2,256,2,256]{3,2,1,0:T(2,128)(2,1)S(1)}, bf16[2,256,2,256]{3,2,1,0:T(2,128)(2,1)}, bf16[2,256,2,256]{3,2,1,0:T(2,128)(2,1)}, bf16[2,256,2,256...) fusion(bf16[18,256,2,256]{3,2,1,0:T(2,128)(2,1)} %broadcast_mul, ...), kind=kLoop, calls=%fused_computation.33 | loop fusion | bytes 9437184 | tf_op jit(solution)/shard_map/slice | solution.py:78
  312.1 3.8 fusion.14
  315.8 7.7 %collective-permute-done.4 = bf16[3,512,512]{2,1,0:T(8,128)(2,1)} collective-permute-done((bf16[3,512,512]{2,1,0:T(8,128)(2,1)}, bf16[3,512,512]{2,1,0:T(8,128)(2,1)}, u32[]{:S(2)}, u32[]{:S(2)}) %collective-permute-start.4) | collective-permute-done | bytes 1572896 | tf_op jit(solution)/shard_map/ppermute | solution.py:11
  323.5 4.0 fusion.15
  327.7 4.0 fusion.16
  331.8 82.2 %all-reduce.2.cloned.1.call-done = bf16[4608,512]{1,0:T(8,128)(2,1)} async-done(((bf16[4608,512]{1,0:T(8,128)(2,1)}), bf16[4608,512]{1,0:T(8,128)(2,1)}) %all-reduce.2.cloned.1.call-update) | async-done | bytes 4718608 | tf_op jit(solution)/shard_map/psum | solution.py:16
  414.0 4.3 fusion.6
  418.3 4.3 fusion.7
  430.7 4.2 fusion.5
  434.8 4.1 fusion.18
  438.9 4.1 fusion.4
  443.0 39.6 %collective-permute-done.6 = bf16[3,512,512]{2,1,0:T(8,128)(2,1)S(1)} collective-permute-done((bf16[3,512,512]{2,1,0:T(8,128)(2,1)}, bf16[3,512,512]{2,1,0:T(8,128)(2,1)S(1)}, u32[]{:S(2)}, u32[]{:S(2)}) %collective-permute-start.6) | collective-permute-done | bytes 1572896 | tf_op jit(solution)/shard_map/ppermute | solution.py:11
  482.6 4.0 fusion.19
  486.9 4.2 fusion.3
  491.1 4.1 fusion.20
  500.5 39.3 %collective-permute-done.7 = bf16[3,512,512]{2,1,0:T(8,128)(2,1)S(1)} collective-permute-done((bf16[3,512,512]{2,1,0:T(8,128)(2,1)S(1)}, bf16[3,512,512]{2,1,0:T(8,128)(2,1)S(1)}, u32[]{:S(2)}, u32[]{:S(2)}) %collective-permute-start.7) | collective-permute-done | bytes 1572896 | tf_op jit(solution)/shard_map/ppermute | solution.py:11
  542.4 23.7 %fusion.1 = bf16[3,512,512]{2,1,0:T(8,128)(2,1)} fusion(f32[3,512,512]{1,2,0:T(8,128)} %fusion.2, f32[3,512,512]{1,2,0:T(8,128)} %fusion.3, f32[3,512,512]{1,2,0:T(8,128)} %fusion.4, bf16[3,512,512]{2,1,0:T(8,128)(2,1)S(1)} %broadcast_multiply_fusion.1, f32[3,512,512]{1,2,0:T(8,128)} %fusion.5, f32[3,512,512]{1,2,0:T(8,128)} %fusion.6, ...), kind=kOutput, calls=%fused_computation.3 | convolution fusion | flops 823394304 | bytes 59768836 | tf_op jit(solution)/shard_map/kr,dkc->drc/dot_general | solution.py:33
  (87 shorter events, 49.2 us)
Async XLA Ops:
  6.5 95.8 %copy-start.12 = (s32[32,32]{1,0:T(8,128)S(1)}, s32[32,32]{1,0:T(8,128)}, u32[]{:S(2)}) copy-start(s32[32,32]{1,0:T(8,128)} %param.6) | copy-start | bytes 12292
  6.5 407.4 %all-reduce.2.cloned.1.call-start = ((), (), s32[]{:S(2)}) async-start(), calls=%async_computation | async-start | bytes 9437184 | tf_op jit(solution)/shard_map/psum | solution.py:16
  9.4 40.3 %collective-permute-start.8 = (bf16[3,512,512]{2,1,0:T(8,128)(2,1)S(1)}, bf16[3,512,512]{2,1,0:T(8,128)(2,1)S(1)}, u32[]{:S(2)}, u32[]{:S(2)}) collective-permute-start(bf16[3,512,512]{2,1,0:T(8,128)(2,1)S(1)} %broadcast_multiply_fusion.1), channel_id=1, source_target_pairs={{0,16},{16,32},{32,48},{48,64},{64,80},{80,96},{96,112},{112,128},... | collective-permute-start | bytes 4718600 | tf_op jit(solution)/shard_map/ppermute | solution.py:11
  11.4 91.0 %collective-permute-start = (bf16[3,512,512]{2,1,0:T(8,128)(2,1)S(1)}, bf16[3,512,512]{2,1,0:T(8,128)(2,1)}, u32[]{:S(2)}, u32[]{:S(2)}) collective-permute-start(bf16[3,512,512]{2,1,0:T(8,128)(2,1)S(1)} %broadcast_multiply_fusion.1), channel_id=1, source_target_pairs={{0,1},{1,2},{2,3},{3,4},{4,5},{5,6},{6,7},{7,8},{8,9},{9,10},{10,1... | collective-permute-start | bytes 4718600 | tf_op jit(solution)/shard_map/ppermute | solution.py:11
  49.7 56.5 %copy-start.8 = (bf16[3,512,512]{2,1,0:T(8,128)(2,1)}, bf16[3,512,512]{2,1,0:T(8,128)(2,1)S(1)}, u32[]{:S(2)}) copy-start(bf16[3,512,512]{2,1,0:T(8,128)(2,1)S(1)} %collective-permute-done.8) | copy-start | bytes 4718596
  49.7 56.5 %collective-permute-start.9 = (bf16[3,512,512]{2,1,0:T(8,128)(2,1)S(1)}, bf16[3,512,512]{2,1,0:T(8,128)(2,1)}, u32[]{:S(2)}, u32[]{:S(2)}) collective-permute-start(bf16[3,512,512]{2,1,0:T(8,128)(2,1)S(1)} %collective-permute-done.8), channel_id=1, source_target_pairs={{0,16},{16,32},{32,48},{48,64},{64,80},{80,96},{96,112},{112,128},... | collective-permute-start | bytes 4718600 | tf_op jit(solution)/shard_map/ppermute | solution.py:11
  102.3 57.5 %collective-permute-start.1 = (bf16[3,512,512]{2,1,0:T(8,128)(2,1)}, bf16[3,512,512]{2,1,0:T(8,128)(2,1)}, u32[]{:S(2)}, u32[]{:S(2)}) collective-permute-start(bf16[3,512,512]{2,1,0:T(8,128)(2,1)} %collective-permute-done), channel_id=1, source_target_pairs={{0,1},{1,2},{2,3},{3,4},{4,5},{5,6},{6,7},{7,8},{8,9},{9,10},{10,1... | collective-permute-start | bytes 4718600 | tf_op jit(solution)/shard_map/ppermute | solution.py:11
  105.1 54.7 %slice-start = ((s8[4718592]{0:T(1024)(128)(4,1)}), s8[4194304]{0:T(1024)(128)(4,1)S(1)}, s32[]{:S(2)}) async-start(s8[4718592]{0:T(1024)(128)(4,1)} %bitcast.68), calls=%async_computation.1 | async-start | bytes 8388608
  105.1 54.7 %slice-start.1 = ((s8[4718592]{0:T(1024)(128)(4,1)}), s8[524288]{0:T(1024)(128)(4,1)S(1)}, s32[]{:S(2)}) async-start(s8[4718592]{0:T(1024)(128)(4,1)} %bitcast.68), calls=%async_computation.2 | async-start | bytes 1048576
  106.1 56.4 %collective-permute-start.10 = (bf16[3,512,512]{2,1,0:T(8,128)(2,1)}, bf16[3,512,512]{2,1,0:T(8,128)(2,1)}, u32[]{:S(2)}, u32[]{:S(2)}) collective-permute-start(bf16[3,512,512]{2,1,0:T(8,128)(2,1)} %collective-permute-done.9), channel_id=1, source_target_pairs={{0,16},{16,32},{32,48},{48,64},{64,80},{80,96},{96,112},{112,128},... | collective-permute-start | bytes 4718600 | tf_op jit(solution)/shard_map/ppermute | solution.py:11
  159.8 66.3 %collective-permute-start.2 = (bf16[3,512,512]{2,1,0:T(8,128)(2,1)}, bf16[3,512,512]{2,1,0:T(8,128)(2,1)S(1)}, u32[]{:S(2)}, u32[]{:S(2)}) collective-permute-start(bf16[3,512,512]{2,1,0:T(8,128)(2,1)} %collective-permute-done.1), channel_id=1, source_target_pairs={{0,1},{1,2},{2,3},{3,4},{4,5},{5,6},{6,7},{7,8},{8,9},{9,10},{10,1... | collective-permute-start | bytes 4718600 | tf_op jit(solution)/shard_map/ppermute | solution.py:11
  162.5 71.5 %collective-permute-start.11 = (bf16[3,512,512]{2,1,0:T(8,128)(2,1)}, bf16[3,512,512]{2,1,0:T(8,128)(2,1)}, u32[]{:S(2)}, u32[]{:S(2)}) collective-permute-start(bf16[3,512,512]{2,1,0:T(8,128)(2,1)} %collective-permute-done.10), channel_id=1, source_target_pairs={{0,16},{16,32},{32,48},{48,64},{64,80},{80,96},{96,112},{112,128},... | collective-permute-start | bytes 4718600 | tf_op jit(solution)/shard_map/ppermute | solution.py:11
  226.1 50.4 %collective-permute-start.3 = (bf16[3,512,512]{2,1,0:T(8,128)(2,1)S(1)}, bf16[3,512,512]{2,1,0:T(8,128)(2,1)}, u32[]{:S(2)}, u32[]{:S(2)}) collective-permute-start(bf16[3,512,512]{2,1,0:T(8,128)(2,1)S(1)} %collective-permute-done.2), channel_id=1, source_target_pairs={{0,1},{1,2},{2,3},{3,4},{4,5},{5,6},{6,7},{7,8},{8,9},{9,10},{10,1... | collective-permute-start | bytes 4718600 | tf_op jit(solution)/shard_map/ppermute | solution.py:11
  234.1 93.5 %collective-permute-start.12 = (bf16[3,512,512]{2,1,0:T(8,128)(2,1)}, bf16[3,512,512]{2,1,0:T(8,128)(2,1)}, u32[]{:S(2)}, u32[]{:S(2)}) collective-permute-start(bf16[3,512,512]{2,1,0:T(8,128)(2,1)} %collective-permute-done.11), channel_id=1, source_target_pairs={{0,128},{16,144},{32,160},{48,176},{64,192},{80,208},{96,224},{112... | collective-permute-start | bytes 4718600 | tf_op jit(solution)/shard_map/ppermute | solution.py:11
  276.5 47.0 %collective-permute-start.4 = (bf16[3,512,512]{2,1,0:T(8,128)(2,1)}, bf16[3,512,512]{2,1,0:T(8,128)(2,1)}, u32[]{:S(2)}, u32[]{:S(2)}) collective-permute-start(bf16[3,512,512]{2,1,0:T(8,128)(2,1)} %collective-permute-done.3), channel_id=1, source_target_pairs={{0,8},{1,9},{2,10},{3,11},{4,12},{5,13},{6,14},{7,15},{8,0},{9,1},... | collective-permute-start | bytes 4718600 | tf_op jit(solution)/shard_map/ppermute | solution.py:11
  299.0 13.1 %copy-start.13 = (s32[3]{0:T(128)S(1)}, s32[3]{0:T(128)}, u32[]{:S(2)}) copy-start(s32[3]{0:T(128)} %param.5) | copy-start | bytes 40
  315.8 11.9 %copy-start.7 = (bf16[512,512,1]{1,0,2:T(8,128)(2,1)S(1)}, bf16[512,512,1]{1,0,2:T(8,128)(2,1)}, u32[]{:S(2)}) copy-start(bf16[512,512,1]{1,0,2:T(8,128)(2,1)} %reshape.27) | copy-start | bytes 1572868
  323.5 101.8 %collective-permute-start.5 = (bf16[3,512,512]{2,1,0:T(8,128)(2,1)}, bf16[3,512,512]{2,1,0:T(8,128)(2,1)}, u32[]{:S(2)}, u32[]{:S(2)}) collective-permute-start(bf16[3,512,512]{2,1,0:T(8,128)(2,1)} %collective-permute-done.4), channel_id=1, source_target_pairs={{0,1},{1,2},{2,3},{3,4},{4,5},{5,6},{6,7},{7,8},{8,9},{9,10},{10,1... | collective-permute-start | bytes 4718600 | tf_op jit(solution)/shard_map/ppermute | solution.py:11
  327.5 100.5 %collective-permute-start.13 = (bf16[3,512,512]{2,1,0:T(8,128)(2,1)}, bf16[3,512,512]{2,1,0:T(8,128)(2,1)}, u32[]{:S(2)}, u32[]{:S(2)}) collective-permute-start(bf16[3,512,512]{2,1,0:T(8,128)(2,1)} %collective-permute-done.12), channel_id=1, source_target_pairs={{0,16},{16,32},{32,48},{48,64},{64,80},{80,96},{96,112},{112,128},... | collective-permute-start | bytes 4718600 | tf_op jit(solution)/shard_map/ppermute | solution.py:11
  425.3 57.4 %collective-permute-start.6 = (bf16[3,512,512]{2,1,0:T(8,128)(2,1)}, bf16[3,512,512]{2,1,0:T(8,128)(2,1)S(1)}, u32[]{:S(2)}, u32[]{:S(2)}) collective-permute-start(bf16[3,512,512]{2,1,0:T(8,128)(2,1)} %collective-permute-done.5), channel_id=1, source_target_pairs={{0,1},{1,2},{2,3},{3,4},{4,5},{5,6},{6,7},{7,8},{8,9},{9,10},{10,1... | collective-permute-start | bytes 4718600 | tf_op jit(solution)/shard_map/ppermute | solution.py:11
  428.0 58.7 %collective-permute-start.14 = (bf16[3,512,512]{2,1,0:T(8,128)(2,1)}, bf16[3,512,512]{2,1,0:T(8,128)(2,1)S(1)}, u32[]{:S(2)}, u32[]{:S(2)}) collective-permute-start(bf16[3,512,512]{2,1,0:T(8,128)(2,1)} %collective-permute-done.13), channel_id=1, source_target_pairs={{0,16},{16,32},{32,48},{48,64},{64,80},{80,96},{96,112},{112,128},... | collective-permute-start | bytes 4718600 | tf_op jit(solution)/shard_map/ppermute | solution.py:11
  438.9 43.7 %copy-start.3 = (bf16[512,512,1]{1,0,2:T(8,128)(2,1)S(1)}, bf16[512,512,1]{1,0,2:T(8,128)(2,1)}, u32[]{:S(2)}) copy-start(bf16[512,512,1]{1,0,2:T(8,128)(2,1)} %reshape.30) | copy-start | bytes 1572868
  482.6 57.2 %collective-permute-start.7 = (bf16[3,512,512]{2,1,0:T(8,128)(2,1)S(1)}, bf16[3,512,512]{2,1,0:T(8,128)(2,1)S(1)}, u32[]{:S(2)}, u32[]{:S(2)}) collective-permute-start(bf16[3,512,512]{2,1,0:T(8,128)(2,1)S(1)} %collective-permute-done.6), channel_id=1, source_target_pairs={{0,1},{1,2},{2,3},{3,4},{4,5},{5,6},{6,7},{7,8},{8,9},{9,10},{10,1... | collective-permute-start | bytes 4718600 | tf_op jit(solution)/shard_map/ppermute | solution.py:11
  486.7 55.7 %collective-permute-start.15 = (bf16[3,512,512]{2,1,0:T(8,128)(2,1)S(1)}, bf16[3,512,512]{2,1,0:T(8,128)(2,1)}, u32[]{:S(2)}, u32[]{:S(2)}) collective-permute-start(bf16[3,512,512]{2,1,0:T(8,128)(2,1)S(1)} %collective-permute-done.14), channel_id=1, source_target_pairs={{0,16},{16,32},{32,48},{48,64},{64,80},{80,96},{96,112},{112,128},... | collective-permute-start | bytes 4718600 | tf_op jit(solution)/shard_map/ppermute | solution.py:11
  (9 other events, 44.9 us)
Sparse Core Ops, SparseCore 0:
  162.7 251.2 all-reduce.1
where the time goes:
time: 583 us; the launch traced here: 573 us
  waiting for transfers between devices  419 us (72%)
  matrix products  84.8 us (15%)
  local copies, waits for them, and re-layouts  36.4 us (6%)
  other arithmetic  13.8 us (2%)
  between operations  13.8 us (2%)
    ppermute x16, waiting for transfers between devices, from_behind(): lax.ppermute(array, axis, [(i, (i + by) % length) for i in range(length)])  336 us
    psum x1, waiting for transfers between devices, broadcast(): return lax.psum(jnp.where(mine, array, jnp.zeros_like(array)), axis)  82.2 us
    dot_general x9, matrix products, left_product(): jnp.einsum('kr,dkc->drc', left_op, right_op, preferred_element_type=jnp.f...  52.9 us
    dot_general x9, matrix products, right_product(): jnp.einsum('drc,ck->drk', left_op, right_op, preferred_element_type=jnp.f...  31.9 us
    slice x10, local copies, waits for them, and re-layouts, col_add(): strip_local[(distance + col_span) * col_width:(distance + col_span + 1) *...  23.8 us
  transfers between devices with their start and end apart: 17, of which 9 were waited for; matrix products, arithmetic and copies ran while one was open for 19% of the time, Pallas kernels for 0%

commit v1 on v0

--- a/solution.py
+++ b/solution.py
@@ -4,6 +4,12 @@
 from jax.sharding import PartitionSpec as P
 
 BLK = 256
+
+
+def add_all(x, axis):
+    pieces = lax.all_gather(x, axis, axis=0, tiled=False)
+    summed = pieces.sum(axis=0)
+    return summed
 
 
 def from_behind(array, axis, by):
@@ -13,7 +19,7 @@
 
 def broadcast(array, axis, root):
     mine = lax.axis_index(axis) == root
-    return lax.psum(jnp.where(mine, array, jnp.zeros_like(array)), axis)
+    return add_all(jnp.where(mine, array, jnp.zeros_like(array)), axis)
 
 
 def mask_blocks(values, occupancy):

time: 583 us -> 862 us (1.48)
  waiting for transfers between devices: 419 us -> 655 us
  other arithmetic: 13.8 us -> 39.3 us
  starting transfers between devices: 5.73 us -> 21.5 us
    ppermute x16, waiting for transfers between devices: 336 us -> 601 us  [from_behind(): lax.ppermute(array, axis, [(i, (i + by) % length) for i in range(length)])]
    psum x1 -> x0, waiting for transfers between devices: 82.2 us -> none  [broadcast(): return lax.psum(jnp.where(mine, array, jnp.zeros_like(array)), axis)]
    all_gather x0 -> x1, waiting for transfers between devices: none -> 54.3 us  [add_all(): pieces = lax.all_gather(x, axis, axis=0, tiled=False)]
    reduce_sum x0 -> x1, other arithmetic: none -> 26.8 us  [add_all(): summed = pieces.sum(axis=0)]
    ppermute x16, starting transfers between devices: 5.73 us -> 21.5 us  [from_behind(): lax.ppermute(array, axis, [(i, (i + by) % length) for i in range(length)])]
  transfers between devices with their start and end apart: 17 -> 17, of which waited for: 9 -> 10; matrix products, arithmetic and copies ran while one was open for 19% -> 14% of each run, Pallas kernels for 0% -> 0%
where the time goes in v1:
time: 862 us; the launch traced here: 851 us
  waiting for transfers between devices  655 us (76%)
  matrix products  79.3 us (9%)
  local copies, waits for them, and re-layouts  41.1 us (5%)
  other arithmetic  39.3 us (5%)
  starting transfers between devices  21.5 us (2%)
  between operations  14 us (2%)
    ppermute x16, waiting for transfers between devices, from_behind(): lax.ppermute(array, axis, [(i, (i + by) % length) for i in range(length)])  601 us
    all_gather x1, waiting for transfers between devices, add_all(): pieces = lax.all_gather(x, axis, axis=0, tiled=False)  54.3 us
    dot_general x9, matrix products, left_product(): jnp.einsum('kr,dkc->drc', left_op, right_op, preferred_element_type=jnp.f...  50.9 us
    dot_general x9, matrix products, right_product(): jnp.einsum('drc,ck->drk', left_op, right_op, preferred_element_type=jnp.f...  28.4 us
    reduce_sum x1, other arithmetic, add_all(): summed = pieces.sum(axis=0)  26.8 us
    slice x10, local copies, waits for them, and re-layouts, col_add(): strip_local[(distance + col_span) * col_width:(distance + col_span + 1) *...  22.6 us
    ppermute x16, starting transfers between devices, from_behind(): lax.ppermute(array, axis, [(i, (i + by) % length) for i in range(length)])  21.5 us
  transfers between devices with their start and end apart: 17, of which 10 were waited for; matrix products, arithmetic and copies ran while one was open for 14% of the time, Pallas kernels for 0%

profile of v1, /device:TPU:2, one launch (start us, length us, event | category | flops | bytes accessed | tf_op | source)
XLA Modules:
  0.0 850.6 jit_solution(3747582813442363438)
XLA Ops:
  18.8 78.7 %collective-permute-done = bf16[3,512,512]{2,1,0:T(8,128)(2,1)S(1)} collective-permute-done((bf16[3,512,512]{2,1,0:T(8,128)(2,1)S(1)}, bf16[3,512,512]{2,1,0:T(8,128)(2,1)S(1)}, u32[]{:S(2)}, u32[]{:S(2)}) %collective-permute-start) | collective-permute-done | bytes 1572896 | tf_op jit(solution)/shard_map/ppermute | solution.py:17
  98.8 76.4 %collective-permute-done.1 = bf16[3,512,512]{2,1,0:T(8,128)(2,1)S(1)} collective-permute-done((bf16[3,512,512]{2,1,0:T(8,128)(2,1)S(1)}, bf16[3,512,512]{2,1,0:T(8,128)(2,1)S(1)}, u32[]{:S(2)}, u32[]{:S(2)}) %collective-permute-start.1) | collective-permute-done | bytes 1572896 | tf_op jit(solution)/shard_map/ppermute | solution.py:17
  176.4 55.5 %collective-permute-done.2 = bf16[3,512,512]{2,1,0:T(8,128)(2,1)S(1)} collective-permute-done((bf16[3,512,512]{2,1,0:T(8,128)(2,1)S(1)}, bf16[3,512,512]{2,1,0:T(8,128)(2,1)S(1)}, u32[]{:S(2)}, u32[]{:S(2)}) %collective-permute-start.2) | collective-permute-done | bytes 1572896 | tf_op jit(solution)/shard_map/ppermute | solution.py:17
  233.1 97.6 %collective-permute-done.3 = bf16[3,512,512]{2,1,0:T(8,128)(2,1)S(1)} collective-permute-done((bf16[3,512,512]{2,1,0:T(8,128)(2,1)S(1)}, bf16[3,512,512]{2,1,0:T(8,128)(2,1)S(1)}, u32[]{:S(2)}, u32[]{:S(2)}) %collective-permute-start.3) | collective-permute-done | bytes 1572896 | tf_op jit(solution)/shard_map/ppermute | solution.py:17
  330.7 2.9 collective-permute-start.4
  335.9 54.8 %collective-permute-done.4 = bf16[3,512,512]{2,1,0:T(8,128)(2,1)} collective-permute-done((bf16[3,512,512]{2,1,0:T(8,128)(2,1)S(1)}, bf16[3,512,512]{2,1,0:T(8,128)(2,1)}, u32[]{:S(2)}, u32[]{:S(2)}) %collective-permute-start.4) | collective-permute-done | bytes 1572896 | tf_op jit(solution)/shard_map/ppermute | solution.py:17
  390.7 14.2 %collective-permute-start.5 = (bf16[3,512,512]{2,1,0:T(8,128)(2,1)}, bf16[3,512,512]{2,1,0:T(8,128)(2,1)}, u32[]{:S(2)}, u32[]{:S(2)}) collective-permute-start(bf16[3,512,512]{2,1,0:T(8,128)(2,1)} %collective-permute-done.4), channel_id=1, source_target_pairs={{0,1},{1,2},{2,3},{3,4},{4,5},{5,6},{6,7},{7,8},{8,9},{9,10},{10,1... | collective-permute-start | bytes 4718600 | tf_op jit(solution)/shard_map/ppermute | solution.py:17
  405.0 7.7 reshape.24
  412.7 47.1 %collective-permute-done.12 = bf16[3,512,512]{2,1,0:T(8,128)(2,1)} collective-permute-done((bf16[3,512,512]{2,1,0:T(8,128)(2,1)S(1)}, bf16[3,512,512]{2,1,0:T(8,128)(2,1)}, u32[]{:S(2)}, u32[]{:S(2)}) %collective-permute-start.12) | collective-permute-done | bytes 1572896 | tf_op jit(solution)/shard_map/ppermute | solution.py:17
  459.8 8.5 %broadcast_multiply_fusion = bf16[18,256,2,256]{3,2,1,0:T(2,128)(2,1)} fusion(bf16[18,256,2,256]{3,2,1,0:T(2,128)(2,1)} %reshape.24, bf16[18,2]{1,0:T(8,128)(2,1)S(1)} %copy.27), kind=kLoop, calls=%fused_computation.5 | loop fusion | flops 2359296 | bytes 9437256 | tf_op jit(solution)/shard_map/mul | solution.py:31
  468.3 66.7 %collective-permute-done.5 = bf16[3,512,512]{2,1,0:T(8,128)(2,1)} collective-permute-done((bf16[3,512,512]{2,1,0:T(8,128)(2,1)}, bf16[3,512,512]{2,1,0:T(8,128)(2,1)}, u32[]{:S(2)}, u32[]{:S(2)}) %collective-permute-start.5) | collective-permute-done | bytes 1572896 | tf_op jit(solution)/shard_map/ppermute | solution.py:17
  535.0 5.9 fusion.13
  566.7 59.5 %collective-permute-done.6 = bf16[3,512,512]{2,1,0:T(8,128)(2,1)} collective-permute-done((bf16[3,512,512]{2,1,0:T(8,128)(2,1)}, bf16[3,512,512]{2,1,0:T(8,128)(2,1)}, u32[]{:S(2)}, u32[]{:S(2)}) %collective-permute-start.6) | collective-permute-done | bytes 1572896 | tf_op jit(solution)/shard_map/ppermute | solution.py:17
  631.5 4.2 fusion.19
  635.7 4.1 fusion.20
  639.8 4.1 fusion.21
  643.9 64.7 %collective-permute-done.7 = bf16[3,512,512]{2,1,0:T(8,128)(2,1)S(1)} collective-permute-done((bf16[3,512,512]{2,1,0:T(8,128)(2,1)}, bf16[3,512,512]{2,1,0:T(8,128)(2,1)S(1)}, u32[]{:S(2)}, u32[]{:S(2)}) %collective-permute-start.7) | collective-permute-done | bytes 1572896 | tf_op jit(solution)/shard_map/ppermute | solution.py:17
  711.3 54.3 %all-gather.3.cloned.1.call-done = bf16[73728,512]{1,0:T(8,128)(2,1)} async-done(((bf16[4608,512]{1,0:T(8,128)(2,1)}), bf16[73728,512]{1,0:T(8,128)(2,1)}) %all-gather.3.cloned.1.call-update) | async-done | bytes 75497488 | tf_op jit(solution)/shard_map/all_gather | solution.py:10
  765.6 26.8 %reduce_sum.12 = bf16[4608,512]{1,0:T(8,128)(2,1)} reduce(bf16[16,4608,512]{2,1,0:T(8,128)(2,1)} %bitcast, bf16[]{:T(256)} %constant.38.clone.1), dimensions={0}, to_apply=%region_0.1 | reduce | flops 35389440 | bytes 80216064 | tf_op jit(solution)/shard_map/reduce_sum | solution.py:11
  792.4 3.9 fusion.9
  796.3 4.1 fusion.2
  800.3 4.1 fusion.3
  804.5 4.3 fusion.4
  819.6 23.7 %fusion.1 = bf16[3,512,512]{2,1,0:T(8,128)(2,1)} fusion(f32[3,512,512]{1,2,0:T(8,128)} %fusion.2, f32[3,512,512]{1,2,0:T(8,128)} %fusion.3, f32[3,512,512]{1,2,0:T(8,128)} %fusion.4, bf16[3,512,512]{2,1,0:T(8,128)(2,1)S(1)} %broadcast_multiply_fusion.1, f32[3,512,512]{1,2,0:T(8,128)} %fusion.5, f32[3,512,512]{1,2,0:T(8,128)} %fusion.6, ...), kind=kOutput, calls=%fused_computation.3 | convolution fusion | flops 823394304 | bytes 59768836 | tf_op jit(solution)/shard_map/kr,dkc->drc/dot_general | solution.py:39
  (114 shorter events, 62.8 us)
Async XLA Ops:
  6.5 759.1 %all-gather.3.cloned.1.call-start = ((), (), s32[]{:S(2)}) async-start(), calls=%async_computation | async-start | bytes 80216064 | tf_op jit(solution)/shard_map/all_gather | solution.py:10
  16.8 80.8 %collective-permute-start = (bf16[3,512,512]{2,1,0:T(8,128)(2,1)S(1)}, bf16[3,512,512]{2,1,0:T(8,128)(2,1)S(1)}, u32[]{:S(2)}, u32[]{:S(2)}) collective-permute-start(bf16[3,512,512]{2,1,0:T(8,128)(2,1)S(1)} %broadcast_multiply_fusion.1), channel_id=1, source_target_pairs={{0,1},{1,2},{2,3},{3,4},{4,5},{5,6},{6,7},{7,8},{8,9},{9,10},{10,1... | collective-permute-start | bytes 4718600 | tf_op jit(solution)/shard_map/ppermute | solution.py:17
  16.8 80.7 %collective-permute-start.8 = (bf16[3,512,512]{2,1,0:T(8,128)(2,1)S(1)}, bf16[3,512,512]{2,1,0:T(8,128)(2,1)S(1)}, u32[]{:S(2)}, u32[]{:S(2)}) collective-permute-start(bf16[3,512,512]{2,1,0:T(8,128)(2,1)S(1)} %broadcast_multiply_fusion.1), channel_id=1, source_target_pairs={{0,16},{16,32},{32,48},{48,64},{64,80},{80,96},{96,112},{112,128},... | collective-permute-start | bytes 4718600 | tf_op jit(solution)/shard_map/ppermute | solution.py:17
  97.6 236.0 %copy-start.18 = (bf16[3,512,512]{2,1,0:T(8,128)(2,1)}, bf16[3,512,512]{2,1,0:T(8,128)(2,1)S(1)}, u32[]{:S(2)}) copy-start(bf16[3,512,512]{2,1,0:T(8,128)(2,1)S(1)} %collective-permute-done) | copy-start | bytes 4718596
  97.6 77.6 %collective-permute-start.1 = (bf16[3,512,512]{2,1,0:T(8,128)(2,1)S(1)}, bf16[3,512,512]{2,1,0:T(8,128)(2,1)S(1)}, u32[]{:S(2)}, u32[]{:S(2)}) collective-permute-start(bf16[3,512,512]{2,1,0:T(8,128)(2,1)S(1)} %collective-permute-done), channel_id=1, source_target_pairs={{0,1},{1,2},{2,3},{3,4},{4,5},{5,6},{6,7},{7,8},{8,9},{9,10},{10,1... | collective-permute-start | bytes 4718600 | tf_op jit(solution)/shard_map/ppermute | solution.py:17
  98.8 76.4 %collective-permute-start.9 = (bf16[3,512,512]{2,1,0:T(8,128)(2,1)S(1)}, bf16[3,512,512]{2,1,0:T(8,128)(2,1)S(1)}, u32[]{:S(2)}, u32[]{:S(2)}) collective-permute-start(bf16[3,512,512]{2,1,0:T(8,128)(2,1)S(1)} %collective-permute-done.8), channel_id=1, source_target_pairs={{0,16},{16,32},{32,48},{48,64},{64,80},{80,96},{96,112},{112,128},... | collective-permute-start | bytes 4718600 | tf_op jit(solution)/shard_map/ppermute | solution.py:17
  175.2 160.7 %copy-start.20 = (bf16[3,512,512]{2,1,0:T(8,128)(2,1)}, bf16[3,512,512]{2,1,0:T(8,128)(2,1)S(1)}, u32[]{:S(2)}) copy-start(bf16[3,512,512]{2,1,0:T(8,128)(2,1)S(1)} %collective-permute-done.1) | copy-start | bytes 4718596
  175.2 56.7 %collective-permute-start.2 = (bf16[3,512,512]{2,1,0:T(8,128)(2,1)S(1)}, bf16[3,512,512]{2,1,0:T(8,128)(2,1)S(1)}, u32[]{:S(2)}, u32[]{:S(2)}) collective-permute-start(bf16[3,512,512]{2,1,0:T(8,128)(2,1)S(1)} %collective-permute-done.1), channel_id=1, source_target_pairs={{0,1},{1,2},{2,3},{3,4},{4,5},{5,6},{6,7},{7,8},{8,9},{9,10},{10,1... | collective-permute-start | bytes 4718600 | tf_op jit(solution)/shard_map/ppermute | solution.py:17
  176.4 55.5 %collective-permute-start.10 = (bf16[3,512,512]{2,1,0:T(8,128)(2,1)S(1)}, bf16[3,512,512]{2,1,0:T(8,128)(2,1)S(1)}, u32[]{:S(2)}, u32[]{:S(2)}) collective-permute-start(bf16[3,512,512]{2,1,0:T(8,128)(2,1)S(1)} %collective-permute-done.9), channel_id=1, source_target_pairs={{0,16},{16,32},{32,48},{48,64},{64,80},{80,96},{96,112},{112,128},... | collective-permute-start | bytes 4718600 | tf_op jit(solution)/shard_map/ppermute | solution.py:17
  231.9 158.8 %copy-start.22 = (bf16[3,512,512]{2,1,0:T(8,128)(2,1)}, bf16[3,512,512]{2,1,0:T(8,128)(2,1)S(1)}, u32[]{:S(2)}) copy-start(bf16[3,512,512]{2,1,0:T(8,128)(2,1)S(1)} %collective-permute-done.2) | copy-start | bytes 4718596
  231.9 98.8 %collective-permute-start.3 = (bf16[3,512,512]{2,1,0:T(8,128)(2,1)S(1)}, bf16[3,512,512]{2,1,0:T(8,128)(2,1)S(1)}, u32[]{:S(2)}, u32[]{:S(2)}) collective-permute-start(bf16[3,512,512]{2,1,0:T(8,128)(2,1)S(1)} %collective-permute-done.2), channel_id=1, source_target_pairs={{0,1},{1,2},{2,3},{3,4},{4,5},{5,6},{6,7},{7,8},{8,9},{9,10},{10,1... | collective-permute-start | bytes 4718600 | tf_op jit(solution)/shard_map/ppermute | solution.py:17
  233.1 100.5 %collective-permute-start.11 = (bf16[3,512,512]{2,1,0:T(8,128)(2,1)S(1)}, bf16[3,512,512]{2,1,0:T(8,128)(2,1)S(1)}, u32[]{:S(2)}, u32[]{:S(2)}) collective-permute-start(bf16[3,512,512]{2,1,0:T(8,128)(2,1)S(1)} %collective-permute-done.10), channel_id=1, source_target_pairs={{0,16},{16,32},{32,48},{48,64},{64,80},{80,96},{96,112},{112,128},... | collective-permute-start | bytes 4718600 | tf_op jit(solution)/shard_map/ppermute | solution.py:17
  330.7 60.0 %collective-permute-start.4 = (bf16[3,512,512]{2,1,0:T(8,128)(2,1)S(1)}, bf16[3,512,512]{2,1,0:T(8,128)(2,1)}, u32[]{:S(2)}, u32[]{:S(2)}) collective-permute-start(bf16[3,512,512]{2,1,0:T(8,128)(2,1)S(1)} %collective-permute-done.3), channel_id=1, source_target_pairs={{0,8},{1,9},{2,10},{3,11},{4,12},{5,13},{6,14},{7,15},{8,0},{9,1},... | collective-permute-start | bytes 4718600 | tf_op jit(solution)/shard_map/ppermute | solution.py:17
  333.6 79.1 %copy-start.16 = (bf16[3,512,512]{2,1,0:T(8,128)(2,1)}, bf16[3,512,512]{2,1,0:T(8,128)(2,1)S(1)}, u32[]{:S(2)}) copy-start(bf16[3,512,512]{2,1,0:T(8,128)(2,1)S(1)} %collective-permute-done.11) | copy-start | bytes 4718596
  333.6 126.2 %collective-permute-start.12 = (bf16[3,512,512]{2,1,0:T(8,128)(2,1)S(1)}, bf16[3,512,512]{2,1,0:T(8,128)(2,1)}, u32[]{:S(2)}, u32[]{:S(2)}) collective-permute-start(bf16[3,512,512]{2,1,0:T(8,128)(2,1)S(1)} %collective-permute-done.11), channel_id=1, source_target_pairs={{0,128},{16,144},{32,160},{48,176},{64,192},{80,208},{96,224},{112... | collective-permute-start | bytes 4718600 | tf_op jit(solution)/shard_map/ppermute | solution.py:17
  390.7 144.3 %collective-permute-start.5 = (bf16[3,512,512]{2,1,0:T(8,128)(2,1)}, bf16[3,512,512]{2,1,0:T(8,128)(2,1)}, u32[]{:S(2)}, u32[]{:S(2)}) collective-permute-start(bf16[3,512,512]{2,1,0:T(8,128)(2,1)} %collective-permute-done.4), channel_id=1, source_target_pairs={{0,1},{1,2},{2,3},{3,4},{4,5},{5,6},{6,7},{7,8},{8,9},{9,10},{10,1... | collective-permute-start | bytes 4718600 | tf_op jit(solution)/shard_map/ppermute | solution.py:17
  459.8 104.2 %collective-permute-start.13 = (bf16[3,512,512]{2,1,0:T(8,128)(2,1)}, bf16[3,512,512]{2,1,0:T(8,128)(2,1)}, u32[]{:S(2)}, u32[]{:S(2)}) collective-permute-start(bf16[3,512,512]{2,1,0:T(8,128)(2,1)} %collective-permute-done.12), channel_id=1, source_target_pairs={{0,16},{16,32},{32,48},{48,64},{64,80},{80,96},{96,112},{112,128},... | collective-permute-start | bytes 4718600 | tf_op jit(solution)/shard_map/ppermute | solution.py:17
  535.0 91.2 %collective-permute-start.6 = (bf16[3,512,512]{2,1,0:T(8,128)(2,1)}, bf16[3,512,512]{2,1,0:T(8,128)(2,1)}, u32[]{:S(2)}, u32[]{:S(2)}) collective-permute-start(bf16[3,512,512]{2,1,0:T(8,128)(2,1)} %collective-permute-done.5), channel_id=1, source_target_pairs={{0,1},{1,2},{2,3},{3,4},{4,5},{5,6},{6,7},{7,8},{8,9},{9,10},{10,1... | collective-permute-start | bytes 4718600 | tf_op jit(solution)/shard_map/ppermute | solution.py:17
  564.0 62.2 %copy-start.5 = (bf16[512,512,1]{1,0,2:T(8,128)(2,1)S(1)}, bf16[512,512,1]{1,0,2:T(8,128)(2,1)}, u32[]{:S(2)}) copy-start(bf16[512,512,1]{1,0,2:T(8,128)(2,1)} %reshape.29) | copy-start | bytes 1572868
  564.0 62.2 %copy-start.23 = (bf16[3,512,512]{2,1,0:T(8,128)(2,1)S(1)}, bf16[3,512,512]{2,1,0:T(8,128)(2,1)}, u32[]{:S(2)}) copy-start(bf16[3,512,512]{2,1,0:T(8,128)(2,1)} %copy-done.22) | copy-start | bytes 4718596
  564.0 75.8 %collective-permute-start.14 = (bf16[3,512,512]{2,1,0:T(8,128)(2,1)}, bf16[3,512,512]{2,1,0:T(8,128)(2,1)}, u32[]{:S(2)}, u32[]{:S(2)}) collective-permute-start(bf16[3,512,512]{2,1,0:T(8,128)(2,1)} %collective-permute-done.13), channel_id=1, source_target_pairs={{0,16},{16,32},{32,48},{48,64},{64,80},{80,96},{96,112},{112,128},... | collective-permute-start | bytes 4718600 | tf_op jit(solution)/shard_map/ppermute | solution.py:17
  566.7 62.2 %copy-start.25 = (bf16[3,512,512]{2,1,0:T(8,128)(2,1)S(1)}, bf16[3,512,512]{2,1,0:T(8,128)(2,1)}, u32[]{:S(2)}) copy-start(bf16[3,512,512]{2,1,0:T(8,128)(2,1)} %copy-done.24) | copy-start | bytes 4718596
  626.2 82.4 %collective-permute-start.7 = (bf16[3,512,512]{2,1,0:T(8,128)(2,1)}, bf16[3,512,512]{2,1,0:T(8,128)(2,1)S(1)}, u32[]{:S(2)}, u32[]{:S(2)}) collective-permute-start(bf16[3,512,512]{2,1,0:T(8,128)(2,1)} %collective-permute-done.6), channel_id=1, source_target_pairs={{0,1},{1,2},{2,3},{3,4},{4,5},{5,6},{6,7},{7,8},{8,9},{9,10},{10,1... | collective-permute-start | bytes 4718600 | tf_op jit(solution)/shard_map/ppermute | solution.py:17
  639.8 179.8 %collective-permute-start.15 = (bf16[3,512,512]{2,1,0:T(8,128)(2,1)}, bf16[3,512,512]{2,1,0:T(8,128)(2,1)}, u32[]{:S(2)}, u32[]{:S(2)}) collective-permute-start(bf16[3,512,512]{2,1,0:T(8,128)(2,1)} %collective-permute-done.14), channel_id=1, source_target_pairs={{0,16},{16,32},{32,48},{48,64},{64,80},{80,96},{96,112},{112,128},... | collective-permute-start | bytes 4718600 | tf_op jit(solution)/shard_map/ppermute | solution.py:17
  (22 other events, 176.7 us)
Sparse Core Ops, SparseCore 0:
  15.3 750.2 all-gather.2
